TPU v7x, 32 devices: a whole 2x2x4 slice. The times are simulated.
32 devices in a mesh: mol: 2 (over x), occ: 16 (over z, y, core).
Axes of the slice: x: 2, y: 2, z: 4, core: 2. Of those that a mesh axis runs over, the one named last changes fastest.
Arguments:
- integrals: bfloat16 [512, 128, 2048], P(('mol', 'occ')), parts along dimension 0, may hold values from -6 to 6
- orbitals: bfloat16 [4096, 1536], P('mol'), parts along dimension 0
- occ_energy: float32 [256], P('mol'), parts along dimension 0, may hold values from -2 to -0.3
- vir_energy: float32 [3072], P('mol'), parts along dimension 0, may hold values from 0.1 to 3
- owner: int32 [16], P('mol'), parts along dimension 0, may hold values from 0 to 127
- vblock: int32 [16], P('mol'), parts along dimension 0, may hold values from 0 to 7
Outputs:
- factors: bfloat16 [512, 128, 1536], P('mol', 'occ'), parts along dimension 0
- pair_energy: float32 [256, 8], P(('mol', 'occ')), parts along dimension 0
There are 2 independent parts, one for each index of `mol`. A program takes and returns all parts, laid end to end along the dimension named above; each array names one. Nothing has to cross between parts.
Inputs may be any that keep to these rules, and one draw needn't show every extreme that they name: `owner`: each step names one occupied orbital and one virtual block; steps may repeat.
All inputs are finite; a program needn't handle non-finite values.
Results may differ from a plain program's by a relative error of at most 0.001.
Values may be sent and summed in bfloat16 or wider, within the bound.
No kernel may reach another device: no remote copies, remote signals or barrier semaphores. Data moves between devices by JAX's collectives and lax.ppermute only.
A program may use at most 128 MiB of HBM per device.

v0:
```python
import jax
import jax.numpy as jnp
from jax import lax
from jax.sharding import PartitionSpec as P

VBLK = 192
EDGE_PART = 4


def chunk_energies(factors, blocks, occ_rows, occ_cols, vir_chunk, vir_blocks, scale):
    coulomb = lax.dot_general(
        factors, blocks, (((0,), (0,)), ((), ())), preferred_element_type=jnp.float32
    )
    rows_part = vir_chunk[None, :] - occ_rows[:, None]
    cols_part = vir_blocks - occ_cols[:, None]
    denom = rows_part[:, :, None, None] + cols_part[None, None, :, :]
    return jnp.sum(coulomb * coulomb / denom, axis=(1, 3))


def per_device(integrals, orbitals, occ_energy, vir_energy, owner, vblock):
    aux_here, occ_total, basis_count = integrals.shape
    nvir = orbitals.shape[1]
    step_count = owner.shape[0]
    groups = lax.psum(1, "occ")
    local_count = occ_total // groups
    tiles = nvir // 128 if nvir % 128 == 0 else 0
    edge = tiles // EDGE_PART
    if edge >= 1 and tiles - 2 * edge >= 1:
        bounds = [0, edge * 128, nvir - edge * 128, nvir]
    else:
        bounds = [0, nvir]
    chunks = len(bounds) - 1
    ride = step_count == local_count
    rows = integrals.reshape(aux_here, groups, local_count, basis_count)
    rows = jnp.transpose(rows, (1, 0, 2, 3))

    def chunk_product(c):
        return lax.dot_general(
            rows,
            orbitals[:, bounds[c] : bounds[c + 1]],
            (((3,), (0,)), ((), ())),
            preferred_element_type=jnp.float32,
        ).astype(jnp.bfloat16)

    first_product = chunk_product(0)
    first_product, late = lax.optimization_barrier((first_product, owner))
    picked = jnp.take(integrals, late, axis=1)
    picked = (
        jnp.dot(
            picked.reshape(aux_here * step_count, basis_count),
            orbitals,
            preferred_element_type=jnp.float32,
        )
        .astype(jnp.bfloat16)
        .reshape(aux_here, step_count, nvir)
    )
    pieces = jnp.stack(
        [
            lax.dynamic_slice_in_dim(picked[:, s, :], vblock[s] * VBLK, VBLK, axis=1)
            for s in range(step_count)
        ],
        axis=1,
    )
    me = lax.axis_index("occ")
    occ_here = lax.dynamic_slice(occ_energy, (me * local_count,), (local_count,))
    occ_cols = occ_energy[owner]
    vir_blocks = jnp.stack(
        [lax.dynamic_slice(vir_energy, (vblock[s] * VBLK,), (VBLK,)) for s in range(step_count)]
    )
    scale = 1.0 / (aux_here * groups * nvir * VBLK)
    carrier = min(1, chunks - 1) if ride else -1
    if not ride:
        blocks = lax.all_gather(pieces, "occ", axis=0, tiled=True)
    raw = []
    sums = []
    made_at = {}
    pending = []
    for c in range(chunks):
        cols = slice(bounds[c], bounds[c + 1])
        span = bounds[c + 1] - bounds[c]
        product = first_product if c == 0 else chunk_product(c)
        if c == carrier:
            extra = jnp.broadcast_to(pieces[None], (groups, aux_here, step_count, VBLK))
            product = jnp.concatenate([product, extra], axis=3)
        if c >= 1:
            held = (raw[-1],) + tuple(made_at.get(c - 2, ()))
            product, _ = lax.optimization_barrier((product, held))
        got = lax.all_to_all(product, "occ", split_axis=0, concat_axis=0, tiled=True)
        raw.append(got)
        got = got.reshape(groups * aux_here, local_count, got.shape[-1])
        if c == carrier:
            blocks = got[:, :, span:]
            got = got[:, :, :span]
        if c == 0:
            factors = jnp.pad(got, ((0, 0), (0, 0), (0, nvir - span)))
        else:
            factors = lax.dynamic_update_slice(factors, got, (0, 0, bounds[c]))
        if c == carrier:
            whole = raw[-1].reshape(groups * aux_here, local_count, span + VBLK)
            vir_here = jnp.concatenate(
                [vir_energy[cols], jnp.full((VBLK,), jnp.inf, vir_energy.dtype)]
            )
        else:
            whole = lax.optimization_barrier(got)
            vir_here = vir_energy[cols]
        pending.append((whole, vir_here))
        if c >= carrier:
            made = [
                chunk_energies(view, blocks, occ_here, occ_cols, vir_k, vir_blocks, scale)
                for view, vir_k in pending
            ]
            pending = []
            if c < chunks - 1:
                factors, made[0] = lax.optimization_barrier((factors, made[0]))
            made_at[c] = made
            sums.extend(made)
    total = sums[0]
    for extra_sum in sums[1:]:
        total = total + extra_sum
    energies = -total * scale
    return (factors, energies)


def solution(mesh):
    placed = (P(("mol", "occ"), None, None), P("mol", None), P("mol"), P("mol"), P("mol"), P("mol"))
    return jax.shard_map(
        per_device,
        mesh=mesh,
        in_specs=placed,
        out_specs=(P("mol", "occ", None), P(("mol", "occ"), None)),
        check_vma=False,
    )
```

profile of v0, /device:TPU:13, one launch (start us, length us, event | category | flops | bytes accessed | tf_op | source)
XLA Modules:
  0.0 197.3 jit_solution(8760700567116603394)
XLA Ops:
  0.6 9.4 %fusion.21 = bf16[16,16,8,384]{3,2,1,0:T(8,128)(2,1)} fusion(bf16[2048,1536]{1,0:T(8,128)(2,1)} %param.7, bf16[16,128,2048]{2,1,0:T(8,128)(2,1)} %param.6), kind=kOutput, calls=%fused_computation.25 | convolution fusion | flops 3222011904 | bytes 11534336 | tf_op jit(solution)/shard_map/dot_general | solution.py:38
  10.1 6.6 %all-to-all-start = ((bf16[16,16,8,384]{3,2,1,0:T(8,128)(2,1)}), bf16[16,16,8,384]{3,2,1,0:T(8,128)(2,1)S(1)}, u32[]{:S(2)}, u32[]{:S(2)}) async-start(bf16[16,16,8,384]{3,2,1,0:T(8,128)(2,1)} %fusion.21), calls=%async_computation | async-start | bytes 3145728 | tf_op jit(solution)/shard_map/all_to_all | solution.py:88
  16.7 0.7 fusion.42
  22.5 2.6 %gather_fusion = bf16[8,16,2048]{2,0,1:T(8,128)(2,1)S(1)} fusion(bf16[16,128,2048]{2,1,0:T(8,128)(2,1)} %param.6, s32[1024]{0:T(1024)S(1)} %pad_clamp_fusion.1), kind=kCustom, calls=%fused_computation | custom fusion | bytes 1048608 | tf_op jit(solution)/shard_map/jit(_take)/gather | solution.py:47
  25.2 3.8 %fusion.15 = bf16[16,8,1536]{2,1,0:T(8,128)(2,1)S(1)} fusion(bf16[2048,1536]{1,0:T(8,128)(2,1)} %param.7, bf16[8,16,2048]{2,0,1:T(8,128)(2,1)S(1)} %gather_fusion, pred[128]{0:T(512)(128)(4,1)S(1)} %broadcast_in_dim.21), kind=kOutput, calls=%fused_computation.23 | convolution fusion | flops 805765120 | bytes 7209088 | tf_op jit(solution)/shard_map/dot_general | solution.py:49
  29.0 0.7 fusion.39
  29.7 0.1 constant_dynamic-slice_fusion
  29.8 0.1 constant_dynamic-slice_fusion.1
  29.9 0.1 constant_dynamic-slice_fusion.2
  30.0 0.1 constant_dynamic-slice_fusion.3
  30.1 0.1 constant_dynamic-slice_fusion.4
  30.2 0.1 constant_dynamic-slice_fusion.5
  30.5 0.2 stack.38
  30.7 10.0 %fusion.16 = bf16[16,16,8,768]{3,2,1,0:T(8,128)(2,1)S(1)} fusion(bf16[2048,1536]{1,0:T(8,128)(2,1)} %param.7, bf16[16,128,2048]{2,1,0:T(8,128)(2,1)} %param.6), kind=kOutput, calls=%fused_computation.24 | convolution fusion | flops 6444023808 | bytes 14680064 | tf_op jit(solution)/shard_map/dot_general | solution.py:38
  40.9 2.6 %pad_maximum_fusion = bf16[16,16,8,960]{3,2,1,0:T(8,128)(2,1)} fusion(bf16[16,16,8,192]{3,2,1,0:T(8,128)(2,1)S(1)} %broadcast_in_dim.25, bf16[16,16,8,768]{3,2,1,0:T(8,128)(2,1)S(1)} %fusion.16), kind=kLoop, calls=%fused_computation.17 | loop fusion | flops 7864320 | bytes 7864320 | tf_op jit(solution)/shard_map/concatenate | solution.py:84
  43.5 9.3 %all-to-all-done = bf16[16,16,8,384]{3,2,1,0:T(8,128)(2,1)S(1)} async-done(((bf16[16,16,8,384]{3,2,1,0:T(8,128)(2,1)}), bf16[16,16,8,384]{3,2,1,0:T(8,128)(2,1)S(1)}, u32[]{:S(2)}, u32[]{:S(2)}) %all-to-all-start) | async-done | bytes 1572896 | tf_op jit(solution)/shard_map/all_to_all | solution.py:88
  52.8 4.9 %all-to-all-start.1 = ((bf16[16,16,8,960]{3,2,1,0:T(8,128)(2,1)}), bf16[16,16,8,960]{3,2,1,0:T(8,128)(2,1)}, u32[]{:S(2)}, u32[]{:S(2)}) async-start(bf16[16,16,8,960]{3,2,1,0:T(8,128)(2,1)} %pad_maximum_fusion), calls=%async_computation.1 | async-start | bytes 8388608 | tf_op jit(solution)/shard_map/all_to_all | solution.py:88
  57.9 0.6 gather_fusion.1
  58.5 0.1 fusion.41
  58.9 9.5 %fusion.24 = bf16[16,16,8,384]{3,2,1,0:T(8,128)(2,1)} fusion(bf16[2048,1536]{1,0:T(8,128)(2,1)} %param.7, bf16[16,128,2048]{2,1,0:T(8,128)(2,1)} %param.6), kind=kOutput, calls=%fused_computation.26 | convolution fusion | flops 3222011904 | bytes 11534336 | tf_op jit(solution)/shard_map/dot_general | solution.py:38
  68.4 3.2 %pad.5 = bf16[256,8,1536]{2,1,0:T(8,128)(2,1)} pad(bf16[256,8,384]{2,1,0:T(8,128)(2,1)S(1)} %bitcast.80, bf16[]{:T(256)} %constant.44.clone.1), padding=0_0x0_0x0_1152 | pad | bytes 7864322 | tf_op jit(solution)/shard_map/jit(_pad)/pad | solution.py:95
  71.5 78.7 %all-to-all-done.1 = bf16[16,16,8,960]{3,2,1,0:T(8,128)(2,1)} async-done(((bf16[16,16,8,960]{3,2,1,0:T(8,128)(2,1)}), bf16[16,16,8,960]{3,2,1,0:T(8,128)(2,1)}, u32[]{:S(2)}, u32[]{:S(2)}) %all-to-all-start.1) | async-done | bytes 3932192 | tf_op jit(solution)/shard_map/all_to_all | solution.py:88
  150.2 4.9 %all-to-all-start.2 = ((bf16[16,16,8,384]{3,2,1,0:T(8,128)(2,1)}), bf16[16,16,8,384]{3,2,1,0:T(8,128)(2,1)S(1)}, u32[]{:S(2)}, u32[]{:S(2)}) async-start(bf16[16,16,8,384]{3,2,1,0:T(8,128)(2,1)} %fusion.24), calls=%async_computation.2 | async-start | bytes 3145728 | tf_op jit(solution)/shard_map/all_to_all | solution.py:88
  155.1 2.3 %slice.117 = bf16[256,8,192]{2,1,0:T(8,128)(2,1)} slice(bf16[256,8,960]{2,1,0:T(8,128)(2,1)} %bitcast.18), slice={[0:256], [0:8], [768:960]} | slice | bytes 1572864 | tf_op jit(solution)/shard_map/slice | solution.py:92
  157.4 2.7 %copy.30 = bf16[256,8,192]{0,2,1:T(8,128)(2,1)} copy(bf16[256,8,192]{2,1,0:T(8,128)(2,1)} %slice.117) | data formatting | bytes 1572864
  160.0 3.8 %slice_dynamic-update-slice_fusion = bf16[256,8,1536]{2,1,0:T(8,128)(2,1)} fusion(bf16[256,8,1536]{2,1,0:T(8,128)(2,1)} %pad.5, bf16[256,8,960]{2,1,0:T(8,128)(2,1)} %bitcast.18), kind=kLoop, calls=%fused_computation.19 | loop fusion | bytes 6291456 | tf_op jit(solution)/shard_map/dynamic_update_slice | solution.py:97
  163.9 4.1 %fusion.1 = f32[8,8]{1,0:T(8,128)S(1)} fusion(f32[8,192]{1,0:T(8,128)S(1)} %broadcast_subtract_fusion.3, f32[8,384]{1,0:T(8,128)S(1)} %get-tuple-element.33, bf16[256,8,384,1]{2,1,0,3:T(8,128)(2,1)S(1)} %bitcast.81, bf16[256,8,192]{0,2,1:T(8,128)(2,1)S(1)} %copy-done.1), kind=kOutput, calls=%fused_computation.6 | convolution fusion | flops 2434793472 | bytes 2377984 | tf_op jit(solution)/shard_map/dot_general | solution.py:11
  168.0 17.1 %fusion = f32[8,8]{1,0:T(8,128)S(1)} fusion(f32[8,192]{1,0:T(8,128)S(1)} %broadcast_subtract_fusion.3, f32[8,960]{1,0:T(8,128)S(1)} %broadcast_subtract_fusion, bf16[256,8,960,1]{2,1,0,3:T(8,128)(2,1)} %bitcast.32, bf16[256,8,192]{0,2,1:T(8,128)(2,1)S(1)} %copy-done.1), kind=kOutput, calls=%fused_computation.3 | convolution fusion | flops 6086983680 | bytes 4755712 | tf_op jit(solution)/shard_map/dot_general | solution.py:11
  185.1 6.2 %all-to-all-done.2 = bf16[16,16,8,384]{3,2,1,0:T(8,128)(2,1)S(1)} async-done(((bf16[16,16,8,384]{3,2,1,0:T(8,128)(2,1)}), bf16[16,16,8,384]{3,2,1,0:T(8,128)(2,1)S(1)}, u32[]{:S(2)}, u32[]{:S(2)}) %all-to-all-start.2) | async-done | bytes 1572896 | tf_op jit(solution)/shard_map/all_to_all | solution.py:88
  191.3 1.3 constant_dynamic-update-slice_fusion
  192.6 4.1 %fusion.2 = f32[8,8]{1,0:T(8,128)S(1)} fusion(f32[8,384]{1,0:T(8,128)S(1)} %get-tuple-element.32, f32[8,192]{1,0:T(8,128)S(1)} %broadcast_subtract_fusion.3, bf16[256,8,384,1]{2,1,0,3:T(8,128)(2,1)S(1)} %bitcast.79, bf16[256,8,192]{0,2,1:T(8,128)(2,1)S(1)} %copy-done.2), kind=kOutput, calls=%fused_computation.7 | convolution fusion | flops 2434793472 | bytes 2377984 | tf_op jit(solution)/shard_map/dot_general | solution.py:11
  196.7 0.6 negate_multiply_fusion
  (29 shorter events, 0.8 us)
Async XLA Ops:
  0.6 21.7 %copy-start.5 = (s32[8]{0:T(128)S(1)}, s32[8]{0:T(128)}, u32[]{:S(2)}) copy-start(s32[8]{0:T(128)} %param.10) | copy-start | bytes 100
  0.6 16.0 %copy-start.4 = (s32[8]{0:T(128)S(1)}, s32[8]{0:T(128)}, u32[]{:S(2)}) copy-start(s32[8]{0:T(128)} %param.11) | copy-start | bytes 100
  10.1 42.7 %all-to-all-start = ((bf16[16,16,8,384]{3,2,1,0:T(8,128)(2,1)}), bf16[16,16,8,384]{3,2,1,0:T(8,128)(2,1)S(1)}, u32[]{:S(2)}, u32[]{:S(2)}) async-start(bf16[16,16,8,384]{3,2,1,0:T(8,128)(2,1)} %fusion.21), calls=%async_computation | async-start | bytes 3145728 | tf_op jit(solution)/shard_map/all_to_all | solution.py:88
  43.5 14.2 %copy-start.3 = (f32[1536]{0:T(1024)S(1)}, f32[1536]{0:T(1024)}, u32[]{:S(2)}) copy-start(f32[1536]{0:T(1024)} %param.9) | copy-start | bytes 18436
  43.5 14.2 %copy-start = (f32[128]{0:T(128)S(1)}, f32[128]{0:T(128)}, u32[]{:S(2)}) copy-start(f32[128]{0:T(128)} %param.8) | copy-start | bytes 1540
  52.8 97.4 %all-to-all-start.1 = ((bf16[16,16,8,960]{3,2,1,0:T(8,128)(2,1)}), bf16[16,16,8,960]{3,2,1,0:T(8,128)(2,1)}, u32[]{:S(2)}, u32[]{:S(2)}) async-start(bf16[16,16,8,960]{3,2,1,0:T(8,128)(2,1)} %pad_maximum_fusion), calls=%async_computation.1 | async-start | bytes 8388608 | tf_op jit(solution)/shard_map/all_to_all | solution.py:88
  150.2 41.1 %all-to-all-start.2 = ((bf16[16,16,8,384]{3,2,1,0:T(8,128)(2,1)}), bf16[16,16,8,384]{3,2,1,0:T(8,128)(2,1)S(1)}, u32[]{:S(2)}, u32[]{:S(2)}) async-start(bf16[16,16,8,384]{3,2,1,0:T(8,128)(2,1)} %fusion.24), calls=%async_computation.2 | async-start | bytes 3145728 | tf_op jit(solution)/shard_map/all_to_all | solution.py:88
  160.0 3.8 %copy-start.1 = (bf16[256,8,192]{0,2,1:T(8,128)(2,1)S(1)}, bf16[256,8,192]{0,2,1:T(8,128)(2,1)}, u32[]{:S(2)}) copy-start(bf16[256,8,192]{0,2,1:T(8,128)(2,1)} %copy.30) | copy-start | bytes 2359300
  168.0 24.6 %copy-start.2 = (bf16[256,8,192]{0,2,1:T(8,128)(2,1)S(1)}, bf16[256,8,192]{0,2,1:T(8,128)(2,1)}, u32[]{:S(2)}) copy-start(bf16[256,8,192]{0,2,1:T(8,128)(2,1)} %copy.30) | copy-start | bytes 2359300
where the time goes:
time: 198 us; the launch traced here: 197 us
  waiting for transfers between devices  94.2 us (48%)
  matrix products  58.1 us (29%)
  local copies, waits for them, and re-layouts  19.3 us (10%)
  starting transfers between devices  16.4 us (8%)
  between operations  5.89 us (3%)
  other arithmetic  3.46 us (2%)
    all_to_all x3, waiting for transfers between devices, per_device(): lax.all_to_all(product, 'occ', split_axis=0, concat_axis=0, tiled=True)  94.2 us
    dot_general x3, matrix products, chunk_product(): lax.dot_general(rows, orbitals[:, bounds[c]:bounds[c + 1]], (((3,), (0,))...  29 us
    dot_general x3, matrix products, chunk_energies(): lax.dot_general(factors, blocks, (((0,), (0,)), ((), ())), preferred_elem...  25.3 us
    all_to_all x3, starting transfers between devices, per_device(): lax.all_to_all(product, 'occ', split_axis=0, concat_axis=0, tiled=True)  16.4 us
    dynamic_update_slice x2, local copies, waits for them, and re-layouts, per_device(): factors = lax.dynamic_update_slice(factors, got, (0, 0, bounds[c]))  5.13 us
  transfers between devices with their start and end apart: 3, of which 3 were waited for; matrix products, arithmetic and copies ran while one was open for 33% of the time, Pallas kernels for 0%

commit v1 on v0

--- a/solution.py
+++ b/solution.py
@@ -85,7 +85,19 @@
         if c >= 1:
             held = (raw[-1],) + tuple(made_at.get(c - 2, ()))
             product, _ = lax.optimization_barrier((product, held))
-        got = lax.all_to_all(product, "occ", split_axis=0, concat_axis=0, tiled=True)
+        ways, here = (lax.axis_size("occ"), lax.axis_index("occ"))
+        width = product.shape[0] // ways
+        shape = list(product.shape)
+        shape[0] = width
+        height = shape[0]
+        shape[0] = height * ways
+        full = jnp.zeros(shape, product.dtype)
+        for mask in range(ways):
+            part = lax.dynamic_slice_in_dim(product, (here ^ mask) * width, width, axis=0)
+            if mask:
+                part = lax.ppermute(part, "occ", [(d, d ^ mask) for d in range(ways)])
+            full = lax.dynamic_update_slice_in_dim(full, part, (here ^ mask) * height, axis=0)
+        got = full
         raw.append(got)
         got = got.reshape(groups * aux_here, local_count, got.shape[-1])
         if c == carrier:

time: 198 us -> 285 us (1.44)
  starting transfers between devices: 16.4 us -> 62.9 us
  waiting for transfers between devices: 94.2 us -> 126 us
  local copies, waits for them, and re-layouts: 19.3 us -> 23.9 us
  other arithmetic: 3.46 us -> 7.15 us
    ppermute x0 -> x45, waiting for transfers between devices: none -> 126 us  [per_device(): part = lax.ppermute(part, 'occ', [(d, d ^ mask) for d in range(ways)])]
    all_to_all x3 -> x0, waiting for transfers between devices: 94.2 us -> none  [per_device(): lax.all_to_all(product, 'occ', split_axis=0, concat_axis=0, tiled=True)]
    ppermute x0 -> x45, starting transfers between devices: none -> 62.9 us  [per_device(): part = lax.ppermute(part, 'occ', [(d, d ^ mask) for d in range(ways)])]
    all_to_all x3 -> x0, starting transfers between devices: 16.4 us -> none  [per_device(): lax.all_to_all(product, 'occ', split_axis=0, concat_axis=0, tiled=True)]
    dynamic_slice x0 -> x3, local copies, waits for them, and re-layouts: none -> 4.57 us  [per_device(): lax.dynamic_slice_in_dim(product, (here ^ mask) * width, width, axis=0)]
    dynamic_update_slice x2, local copies, waits for them, and re-layouts: 5.13 us -> 0.67 us  [per_device(): factors = lax.dynamic_update_slice(factors, got, (0, 0, bounds[c]))]
    unnamed x13 -> x71, local copies, waits for them, and re-layouts: 2.67 us -> 5.88 us
  transfers between devices with their start and end apart: 3 -> 45, of which waited for: 3 -> 25; matrix products, arithmetic and copies ran while one was open for 33% -> 22% of each run, Pallas kernels for 0% -> 0%
where the time goes in v1:
time: 285 us; the launch traced here: 283 us
  waiting for transfers between devices  126 us (44%)
  starting transfers between devices  62.9 us (22%)
  matrix products  56.8 us (20%)
  local copies, waits for them, and re-layouts  23.9 us (8%)
  other arithmetic  7.15 us (3%)
  between operations  6.76 us (2%)
    ppermute x45, waiting for transfers between devices, per_device(): part = lax.ppermute(part, 'occ', [(d, d ^ mask) for d in range(ways)])  126 us
    ppermute x45, starting transfers between devices, per_device(): part = lax.ppermute(part, 'occ', [(d, d ^ mask) for d in range(ways)])  62.9 us
    dot_general x3, matrix products, chunk_product(): lax.dot_general(rows, orbitals[:, bounds[c]:bounds[c + 1]], (((3,), (0,))...  28.9 us
    dot_general x3, matrix products, chunk_energies(): lax.dot_general(factors, blocks, (((0,), (0,)), ((), ())), preferred_elem...  24.1 us
    unnamed x71, local copies, waits for them, and re-layouts  5.88 us
  transfers between devices with their start and end apart: 45, of which 25 were waited for; matrix products, arithmetic and copies ran while one was open for 22% of the time, Pallas kernels for 0%

profile of v1, /device:TPU:13, one launch (start us, length us, event | category | flops | bytes accessed | tf_op | source)
XLA Modules:
  0.0 283.3 jit_solution(6829553262129051603)
XLA Ops:
  0.7 8.3 %fusion.21 = bf16[16,16,8,384]{3,2,1,0:T(8,128)(2,1)S(1)} fusion(bf16[2048,1536]{1,0:T(8,128)(2,1)} %param.7, bf16[16,128,2048]{2,1,0:T(8,128)(2,1)} %param.6), kind=kOutput, calls=%fused_computation.25 | convolution fusion | flops 3222011904 | bytes 11534336 | tf_op jit(solution)/shard_map/dot_general | solution.py:38
  20.3 11.2 %fusion.16 = bf16[16,16,8,768]{3,2,1,0:T(8,128)(2,1)} fusion(bf16[2048,1536]{1,0:T(8,128)(2,1)} %param.7, bf16[16,128,2048]{2,1,0:T(8,128)(2,1)} %param.6), kind=kOutput, calls=%fused_computation.24 | convolution fusion | flops 6444023808 | bytes 14680064 | tf_op jit(solution)/shard_map/dot_general | solution.py:38
  31.9 9.5 %fusion.24 = bf16[16,16,8,384]{3,2,1,0:T(8,128)(2,1)} fusion(bf16[2048,1536]{1,0:T(8,128)(2,1)} %param.7, bf16[16,128,2048]{2,1,0:T(8,128)(2,1)} %param.6), kind=kOutput, calls=%fused_computation.26 | convolution fusion | flops 3222011904 | bytes 11534336 | tf_op jit(solution)/shard_map/dot_general | solution.py:38
  41.4 2.6 gather_fusion
  44.1 3.8 %fusion.15 = bf16[16,8,1536]{2,1,0:T(8,128)(2,1)S(1)} fusion(bf16[2048,1536]{1,0:T(8,128)(2,1)} %param.7, bf16[8,16,2048]{2,0,1:T(8,128)(2,1)S(1)} %gather_fusion, pred[128]{0:T(512)(128)(4,1)S(1)} %broadcast_in_dim.24), kind=kOutput, calls=%fused_computation.23 | convolution fusion | flops 805765120 | bytes 7209088 | tf_op jit(solution)/shard_map/dot_general | solution.py:49
  49.6 4.6 %pad_maximum_fusion = bf16[16,16,8,960]{3,2,1,0:T(8,128)(2,1)} fusion(bf16[16,16,8,192]{3,2,1,0:T(8,128)(2,1)S(1)} %broadcast_in_dim.50, bf16[16,16,8,768]{3,2,1,0:T(8,128)(2,1)} %fusion.16), kind=kLoop, calls=%fused_computation.17 | loop fusion | flops 7864320 | bytes 7864320 | tf_op jit(solution)/shard_map/concatenate | solution.py:84
  56.5 2.6 collective-permute-start.6
  67.1 7.2 %collective-permute-done.7 = bf16[1,16,8,384]{3,2,1,0:T(8,128)(2,1)S(1)} collective-permute-done((bf16[1,16,8,384]{3,2,1,0:T(8,128)(2,1)S(1)}, bf16[1,16,8,384]{3,2,1,0:T(8,128)(2,1)S(1)}, u32[]{:S(2)}, u32[]{:S(2)}) %collective-permute-start.7) | collective-permute-done | bytes 98336 | tf_op jit(solution)/shard_map/ppermute | solution.py:98
  80.1 4.7 %collective-permute-done.10 = bf16[1,16,8,384]{3,2,1,0:T(8,128)(2,1)S(1)} collective-permute-done((bf16[1,16,8,384]{3,2,1,0:T(8,128)(2,1)S(1)}, bf16[1,16,8,384]{3,2,1,0:T(8,128)(2,1)S(1)}, u32[]{:S(2)}, u32[]{:S(2)}) %collective-permute-start.10) | collective-permute-done | bytes 98336 | tf_op jit(solution)/shard_map/ppermute | solution.py:98
  84.8 4.8 %collective-permute-done.11 = bf16[1,16,8,384]{3,2,1,0:T(8,128)(2,1)S(1)} collective-permute-done((bf16[1,16,8,384]{3,2,1,0:T(8,128)(2,1)S(1)}, bf16[1,16,8,384]{3,2,1,0:T(8,128)(2,1)S(1)}, u32[]{:S(2)}, u32[]{:S(2)}) %collective-permute-start.11) | collective-permute-done | bytes 98336 | tf_op jit(solution)/shard_map/ppermute | solution.py:98
  105.0 3.6 %pad.5 = bf16[256,8,1536]{2,1,0:T(8,128)(2,1)} pad(bf16[256,8,384]{2,1,0:T(8,128)(2,1)S(1)} %bitcast.85, bf16[]{:T(256)} %constant.29.clone.1), padding=0_0x0_0x0_1152 | pad | bytes 7864322 | tf_op jit(solution)/shard_map/jit(_pad)/pad | solution.py:107
  112.4 3.1 %collective-permute-done.17 = bf16[1,16,8,960]{3,2,1,0:T(8,128)(2,1)S(1)} collective-permute-done((bf16[1,16,8,960]{3,2,1,0:T(8,128)(2,1)}, bf16[1,16,8,960]{3,2,1,0:T(8,128)(2,1)S(1)}, u32[]{:S(2)}, u32[]{:S(2)}) %collective-permute-start.17) | collective-permute-done | bytes 245792 | tf_op jit(solution)/shard_map/ppermute | solution.py:98
  115.6 2.5 collective-permute-start.23
  119.9 12.5 %collective-permute-done.20 = bf16[1,16,8,960]{3,2,1,0:T(8,128)(2,1)S(1)} collective-permute-done((bf16[1,16,8,960]{3,2,1,0:T(8,128)(2,1)S(1)}, bf16[1,16,8,960]{3,2,1,0:T(8,128)(2,1)S(1)}, u32[]{:S(2)}, u32[]{:S(2)}) %collective-permute-start.20) | collective-permute-done | bytes 245792 | tf_op jit(solution)/shard_map/ppermute | solution.py:98
  132.5 4.8 %collective-permute-start.25 = (bf16[1,16,8,960]{3,2,1,0:T(8,128)(2,1)S(1)}, bf16[1,16,8,960]{3,2,1,0:T(8,128)(2,1)S(1)}, u32[]{:S(2)}, u32[]{:S(2)}) collective-permute-start(bf16[1,16,8,960]{3,2,1,0:T(8,128)(2,1)S(1)} %get-tuple-element.18), channel_id=1, source_target_pairs={{0,11},{1,10},{2,9},{3,8},{4,15},{5,14},{6,13},{7,12},{8,3},{9,2},... | collective-permute-start | bytes 737288 | tf_op jit(solution)/shard_map/ppermute | solution.py:98
  142.9 29.4 %collective-permute-done.24 = bf16[1,16,8,960]{3,2,1,0:T(8,128)(2,1)S(1)} collective-permute-done((bf16[1,16,8,960]{3,2,1,0:T(8,128)(2,1)S(1)}, bf16[1,16,8,960]{3,2,1,0:T(8,128)(2,1)S(1)}, u32[]{:S(2)}, u32[]{:S(2)}) %collective-permute-start.24) | collective-permute-done | bytes 245792 | tf_op jit(solution)/shard_map/ppermute | solution.py:98
  172.3 2.8 collective-permute-start.29
  175.1 2.8 collective-permute-done.25
  177.9 13.2 %collective-permute-done.26 = bf16[1,16,8,960]{3,2,1,0:T(8,128)(2,1)S(1)} collective-permute-done((bf16[1,16,8,960]{3,2,1,0:T(8,128)(2,1)S(1)}, bf16[1,16,8,960]{3,2,1,0:T(8,128)(2,1)S(1)}, u32[]{:S(2)}, u32[]{:S(2)}) %collective-permute-start.26) | collective-permute-done | bytes 245792 | tf_op jit(solution)/shard_map/ppermute | solution.py:98
  191.1 5.6 %collective-permute-done.27 = bf16[1,16,8,960]{3,2,1,0:T(8,128)(2,1)S(1)} collective-permute-done((bf16[1,16,8,960]{3,2,1,0:T(8,128)(2,1)S(1)}, bf16[1,16,8,960]{3,2,1,0:T(8,128)(2,1)S(1)}, u32[]{:S(2)}, u32[]{:S(2)}) %collective-permute-start.27) | collective-permute-done | bytes 245792 | tf_op jit(solution)/shard_map/ppermute | solution.py:98
  196.8 6.9 %collective-permute-done.28 = bf16[1,16,8,960]{3,2,1,0:T(8,128)(2,1)S(1)} collective-permute-done((bf16[1,16,8,960]{3,2,1,0:T(8,128)(2,1)S(1)}, bf16[1,16,8,960]{3,2,1,0:T(8,128)(2,1)S(1)}, u32[]{:S(2)}, u32[]{:S(2)}) %collective-permute-start.28) | collective-permute-done | bytes 245792 | tf_op jit(solution)/shard_map/ppermute | solution.py:98
  203.7 5.6 %collective-permute-done.29 = bf16[1,16,8,960]{3,2,1,0:T(8,128)(2,1)S(1)} collective-permute-done((bf16[1,16,8,960]{3,2,1,0:T(8,128)(2,1)S(1)}, bf16[1,16,8,960]{3,2,1,0:T(8,128)(2,1)S(1)}, u32[]{:S(2)}, u32[]{:S(2)}) %collective-permute-start.29) | collective-permute-done | bytes 245792 | tf_op jit(solution)/shard_map/ppermute | solution.py:98
  219.2 15.9 %fusion = f32[8,8]{1,0:T(8,128)S(1)} fusion(f32[8,192]{1,0:T(8,128)S(1)} %broadcast_subtract_fusion.3, f32[8,960]{1,0:T(8,128)S(1)} %copy-done.20, bf16[256,8,960,1]{2,1,0,3:T(8,128)(2,1)S(1)} %bitcast.79, bf16[256,8,192]{0,2,1:T(8,128)(2,1)} %copy.31), kind=kOutput, calls=%fused_computation.3 | convolution fusion | flops 6086983680 | bytes 4755712 | tf_op jit(solution)/shard_map/dot_general | solution.py:11
  235.1 4.1 %fusion.1 = f32[8,8]{1,0:T(8,128)S(1)} fusion(f32[8,192]{1,0:T(8,128)S(1)} %broadcast_subtract_fusion.3, f32[8,384]{1,0:T(8,128)S(1)} %copy-done.23, bf16[256,8,384,1]{2,1,0,3:T(8,128)(2,1)S(1)} %bitcast.86, bf16[256,8,192]{0,2,1:T(8,128)(2,1)S(1)} %copy-done.9), kind=kOutput, calls=%fused_computation.6 | convolution fusion | flops 2434793472 | bytes 2377984 | tf_op jit(solution)/shard_map/dot_general | solution.py:11
  239.8 2.7 collective-permute-start.36
  242.7 2.6 collective-permute-start.38
  245.4 3.6 %collective-permute-start.40 = (bf16[1,16,8,384]{3,2,1,0:T(8,128)(2,1)S(1)}, bf16[1,16,8,384]{3,2,1,0:T(8,128)(2,1)S(1)}, u32[]{:S(2)}, u32[]{:S(2)}) collective-permute-start(bf16[1,16,8,384]{3,2,1,0:T(8,128)(2,1)S(1)} %get-tuple-element.34), channel_id=1, source_target_pairs={{0,11},{1,10},{2,9},{3,8},{4,15},{5,14},{6,13},{7,12},{8,3},{9,2},... | collective-permute-start | bytes 294920 | tf_op jit(solution)/shard_map/ppermute | solution.py:98
  249.2 8.3 %collective-permute-start.42 = (bf16[1,16,8,384]{3,2,1,0:T(8,128)(2,1)S(1)}, bf16[1,16,8,384]{3,2,1,0:T(8,128)(2,1)S(1)}, u32[]{:S(2)}, u32[]{:S(2)}) collective-permute-start(bf16[1,16,8,384]{3,2,1,0:T(8,128)(2,1)S(1)} %get-tuple-element.32), channel_id=1, source_target_pairs={{0,13},{1,12},{2,15},{3,14},{4,9},{5,8},{6,11},{7,10},{8,5},{9,4},... | collective-permute-start | bytes 294920 | tf_op jit(solution)/shard_map/ppermute | solution.py:98
  259.3 2.9 %collective-permute-done.39 = bf16[1,16,8,384]{3,2,1,0:T(8,128)(2,1)S(1)} collective-permute-done((bf16[1,16,8,384]{3,2,1,0:T(8,128)(2,1)S(1)}, bf16[1,16,8,384]{3,2,1,0:T(8,128)(2,1)S(1)}, u32[]{:S(2)}, u32[]{:S(2)}) %collective-permute-start.39) | collective-permute-done | bytes 98336 | tf_op jit(solution)/shard_map/ppermute | solution.py:98
  264.3 7.9 %collective-permute-done.41 = bf16[1,16,8,384]{3,2,1,0:T(8,128)(2,1)S(1)} collective-permute-done((bf16[1,16,8,384]{3,2,1,0:T(8,128)(2,1)S(1)}, bf16[1,16,8,384]{3,2,1,0:T(8,128)(2,1)S(1)}, u32[]{:S(2)}, u32[]{:S(2)}) %collective-permute-start.41) | collective-permute-done | bytes 98336 | tf_op jit(solution)/shard_map/ppermute | solution.py:98
  275.8 2.4 collective-permute-done.44
  278.6 4.1 %fusion.2 = f32[8,8]{1,0:T(8,128)S(1)} fusion(f32[8,384]{1,0:T(8,128)S(1)} %get-tuple-element.80, f32[8,192]{1,0:T(8,128)S(1)} %broadcast_subtract_fusion.3, bf16[256,8,384,1]{2,1,0,3:T(8,128)(2,1)S(1)} %bitcast.82, bf16[256,8,192]{0,2,1:T(8,128)(2,1)S(1)} %copy-done.9), kind=kOutput, calls=%fused_computation.7 | convolution fusion | flops 2434793472 | bytes 2377984 | tf_op jit(solution)/shard_map/dot_general | solution.py:11
  (220 shorter events, 69.9 us)
Async XLA Ops:
  10.4 46.0 %collective-permute-start = (bf16[1,16,8,384]{3,2,1,0:T(8,128)(2,1)}, bf16[1,16,8,384]{3,2,1,0:T(8,128)(2,1)S(1)}, u32[]{:S(2)}, u32[]{:S(2)}) collective-permute-start(bf16[1,16,8,384]{3,2,1,0:T(8,128)(2,1)} %get-tuple-element.60), channel_id=1, source_target_pairs={{0,1},{1,0},{2,3},{3,2},{4,5},{5,4},{6,7},{7,6},{8,9},{9,8},{10,11... | collective-permute-start | bytes 294920 | tf_op jit(solution)/shard_map/ppermute | solution.py:98
  11.1 45.4 %collective-permute-start.1 = (bf16[1,16,8,384]{3,2,1,0:T(8,128)(2,1)}, bf16[1,16,8,384]{3,2,1,0:T(8,128)(2,1)S(1)}, u32[]{:S(2)}, u32[]{:S(2)}) collective-permute-start(bf16[1,16,8,384]{3,2,1,0:T(8,128)(2,1)} %get-tuple-element.59), channel_id=1, source_target_pairs={{0,2},{1,3},{2,0},{3,1},{4,6},{5,7},{6,4},{7,5},{8,10},{9,11},{10,... | collective-permute-start | bytes 294920 | tf_op jit(solution)/shard_map/ppermute | solution.py:98
  11.3 47.8 %collective-permute-start.2 = (bf16[1,16,8,384]{3,2,1,0:T(8,128)(2,1)}, bf16[1,16,8,384]{3,2,1,0:T(8,128)(2,1)S(1)}, u32[]{:S(2)}, u32[]{:S(2)}) collective-permute-start(bf16[1,16,8,384]{3,2,1,0:T(8,128)(2,1)} %get-tuple-element.58), channel_id=1, source_target_pairs={{0,3},{1,2},{2,1},{3,0},{4,7},{5,6},{6,5},{7,4},{8,11},{9,10},{10,... | collective-permute-start | bytes 294920 | tf_op jit(solution)/shard_map/ppermute | solution.py:98
  12.7 48.8 %collective-permute-start.3 = (bf16[1,16,8,384]{3,2,1,0:T(8,128)(2,1)}, bf16[1,16,8,384]{3,2,1,0:T(8,128)(2,1)S(1)}, u32[]{:S(2)}, u32[]{:S(2)}) collective-permute-start(bf16[1,16,8,384]{3,2,1,0:T(8,128)(2,1)} %get-tuple-element.57), channel_id=1, source_target_pairs={{0,4},{1,5},{2,6},{3,7},{4,0},{5,1},{6,2},{7,3},{8,12},{9,13},{10,... | collective-permute-start | bytes 294920 | tf_op jit(solution)/shard_map/ppermute | solution.py:98
  12.9 49.2 %collective-permute-start.4 = (bf16[1,16,8,384]{3,2,1,0:T(8,128)(2,1)}, bf16[1,16,8,384]{3,2,1,0:T(8,128)(2,1)S(1)}, u32[]{:S(2)}, u32[]{:S(2)}) collective-permute-start(bf16[1,16,8,384]{3,2,1,0:T(8,128)(2,1)} %get-tuple-element.56), channel_id=1, source_target_pairs={{0,5},{1,4},{2,7},{3,6},{4,1},{5,0},{6,3},{7,2},{8,13},{9,12},{10,... | collective-permute-start | bytes 294920 | tf_op jit(solution)/shard_map/ppermute | solution.py:98
  62.1 16.4 %collective-permute-start.9 = (bf16[1,16,8,384]{3,2,1,0:T(8,128)(2,1)S(1)}, bf16[1,16,8,384]{3,2,1,0:T(8,128)(2,1)S(1)}, u32[]{:S(2)}, u32[]{:S(2)}) collective-permute-start(bf16[1,16,8,384]{3,2,1,0:T(8,128)(2,1)S(1)} %copy-done.15), channel_id=1, source_target_pairs={{0,10},{1,11},{2,8},{3,9},{4,14},{5,15},{6,12},{7,13},{8,2},{9,3},... | collective-permute-start | bytes 294920 | tf_op jit(solution)/shard_map/ppermute | solution.py:98
  64.4 20.4 %collective-permute-start.10 = (bf16[1,16,8,384]{3,2,1,0:T(8,128)(2,1)S(1)}, bf16[1,16,8,384]{3,2,1,0:T(8,128)(2,1)S(1)}, u32[]{:S(2)}, u32[]{:S(2)}) collective-permute-start(bf16[1,16,8,384]{3,2,1,0:T(8,128)(2,1)S(1)} %copy-done.14), channel_id=1, source_target_pairs={{0,11},{1,10},{2,9},{3,8},{4,15},{5,14},{6,13},{7,12},{8,3},{9,2},... | collective-permute-start | bytes 294920 | tf_op jit(solution)/shard_map/ppermute | solution.py:98
  65.8 23.9 %collective-permute-start.11 = (bf16[1,16,8,384]{3,2,1,0:T(8,128)(2,1)S(1)}, bf16[1,16,8,384]{3,2,1,0:T(8,128)(2,1)S(1)}, u32[]{:S(2)}, u32[]{:S(2)}) collective-permute-start(bf16[1,16,8,384]{3,2,1,0:T(8,128)(2,1)S(1)} %get-tuple-element.49), channel_id=1, source_target_pairs={{0,12},{1,13},{2,14},{3,15},{4,8},{5,9},{6,10},{7,11},{8,4},{9,5},... | collective-permute-start | bytes 294920 | tf_op jit(solution)/shard_map/ppermute | solution.py:98
  74.3 17.5 %collective-permute-start.12 = (bf16[1,16,8,384]{3,2,1,0:T(8,128)(2,1)S(1)}, bf16[1,16,8,384]{3,2,1,0:T(8,128)(2,1)S(1)}, u32[]{:S(2)}, u32[]{:S(2)}) collective-permute-start(bf16[1,16,8,384]{3,2,1,0:T(8,128)(2,1)S(1)} %get-tuple-element.48), channel_id=1, source_target_pairs={{0,13},{1,12},{2,15},{3,14},{4,9},{5,8},{6,11},{7,10},{8,5},{9,4},... | collective-permute-start | bytes 294920 | tf_op jit(solution)/shard_map/ppermute | solution.py:98
  76.4 17.4 %collective-permute-start.13 = (bf16[1,16,8,384]{3,2,1,0:T(8,128)(2,1)S(1)}, bf16[1,16,8,384]{3,2,1,0:T(8,128)(2,1)S(1)}, u32[]{:S(2)}, u32[]{:S(2)}) collective-permute-start(bf16[1,16,8,384]{3,2,1,0:T(8,128)(2,1)S(1)} %get-tuple-element.47), channel_id=1, source_target_pairs={{0,14},{1,15},{2,12},{3,13},{4,10},{5,11},{6,8},{7,9},{8,6},{9,7},... | collective-permute-start | bytes 294920 | tf_op jit(solution)/shard_map/ppermute | solution.py:98
  78.5 17.4 %collective-permute-start.14 = (bf16[1,16,8,384]{3,2,1,0:T(8,128)(2,1)S(1)}, bf16[1,16,8,384]{3,2,1,0:T(8,128)(2,1)S(1)}, u32[]{:S(2)}, u32[]{:S(2)}) collective-permute-start(bf16[1,16,8,384]{3,2,1,0:T(8,128)(2,1)S(1)} %get-tuple-element.46), channel_id=1, source_target_pairs={{0,15},{1,14},{2,13},{3,12},{4,11},{5,10},{6,9},{7,8},{8,7},{9,6},... | collective-permute-start | bytes 294920 | tf_op jit(solution)/shard_map/ppermute | solution.py:98
  108.7 23.8 %collective-permute-start.20 = (bf16[1,16,8,960]{3,2,1,0:T(8,128)(2,1)S(1)}, bf16[1,16,8,960]{3,2,1,0:T(8,128)(2,1)S(1)}, u32[]{:S(2)}, u32[]{:S(2)}) collective-permute-start(bf16[1,16,8,960]{3,2,1,0:T(8,128)(2,1)S(1)} %copy-done.13), channel_id=1, source_target_pairs={{0,6},{1,7},{2,4},{3,5},{4,2},{5,3},{6,0},{7,1},{8,14},{9,15},{10,... | collective-permute-start | bytes 737288 | tf_op jit(solution)/shard_map/ppermute | solution.py:98
  110.4 27.7 %collective-permute-start.21 = (bf16[1,16,8,960]{3,2,1,0:T(8,128)(2,1)S(1)}, bf16[1,16,8,960]{3,2,1,0:T(8,128)(2,1)S(1)}, u32[]{:S(2)}, u32[]{:S(2)}) collective-permute-start(bf16[1,16,8,960]{3,2,1,0:T(8,128)(2,1)S(1)} %copy-done.12), channel_id=1, source_target_pairs={{0,7},{1,6},{2,5},{3,4},{4,3},{5,2},{6,1},{7,0},{8,15},{9,14},{10,... | collective-permute-start | bytes 737288 | tf_op jit(solution)/shard_map/ppermute | solution.py:98
  115.6 24.1 %collective-permute-start.22 = (bf16[1,16,8,960]{3,2,1,0:T(8,128)(2,1)S(1)}, bf16[1,16,8,960]{3,2,1,0:T(8,128)(2,1)S(1)}, u32[]{:S(2)}, u32[]{:S(2)}) collective-permute-start(bf16[1,16,8,960]{3,2,1,0:T(8,128)(2,1)S(1)} %copy-done.11), channel_id=1, source_target_pairs={{0,8},{1,9},{2,10},{3,11},{4,12},{5,13},{6,14},{7,15},{8,0},{9,1},... | collective-permute-start | bytes 737288 | tf_op jit(solution)/shard_map/ppermute | solution.py:98
  115.6 25.7 %collective-permute-start.23 = (bf16[1,16,8,960]{3,2,1,0:T(8,128)(2,1)S(1)}, bf16[1,16,8,960]{3,2,1,0:T(8,128)(2,1)S(1)}, u32[]{:S(2)}, u32[]{:S(2)}) collective-permute-start(bf16[1,16,8,960]{3,2,1,0:T(8,128)(2,1)S(1)} %copy-done.10), channel_id=1, source_target_pairs={{0,9},{1,8},{2,11},{3,10},{4,13},{5,12},{6,15},{7,14},{8,1},{9,0},... | collective-permute-start | bytes 737288 | tf_op jit(solution)/shard_map/ppermute | solution.py:98
  118.1 54.2 %collective-permute-start.24 = (bf16[1,16,8,960]{3,2,1,0:T(8,128)(2,1)S(1)}, bf16[1,16,8,960]{3,2,1,0:T(8,128)(2,1)S(1)}, u32[]{:S(2)}, u32[]{:S(2)}) collective-permute-start(bf16[1,16,8,960]{3,2,1,0:T(8,128)(2,1)S(1)} %get-tuple-element.19), channel_id=1, source_target_pairs={{0,10},{1,11},{2,8},{3,9},{4,14},{5,15},{6,12},{7,13},{8,2},{9,3},... | collective-permute-start | bytes 737288 | tf_op jit(solution)/shard_map/ppermute | solution.py:98
  132.5 45.4 %collective-permute-start.25 = (bf16[1,16,8,960]{3,2,1,0:T(8,128)(2,1)S(1)}, bf16[1,16,8,960]{3,2,1,0:T(8,128)(2,1)S(1)}, u32[]{:S(2)}, u32[]{:S(2)}) collective-permute-start(bf16[1,16,8,960]{3,2,1,0:T(8,128)(2,1)S(1)} %get-tuple-element.18), channel_id=1, source_target_pairs={{0,11},{1,10},{2,9},{3,8},{4,15},{5,14},{6,13},{7,12},{8,3},{9,2},... | collective-permute-start | bytes 737288 | tf_op jit(solution)/shard_map/ppermute | solution.py:98
  138.1 53.0 %collective-permute-start.26 = (bf16[1,16,8,960]{3,2,1,0:T(8,128)(2,1)S(1)}, bf16[1,16,8,960]{3,2,1,0:T(8,128)(2,1)S(1)}, u32[]{:S(2)}, u32[]{:S(2)}) collective-permute-start(bf16[1,16,8,960]{3,2,1,0:T(8,128)(2,1)S(1)} %get-tuple-element.17), channel_id=1, source_target_pairs={{0,12},{1,13},{2,14},{3,15},{4,8},{5,9},{6,10},{7,11},{8,4},{9,5},... | collective-permute-start | bytes 737288 | tf_op jit(solution)/shard_map/ppermute | solution.py:98
  139.6 57.1 %collective-permute-start.27 = (bf16[1,16,8,960]{3,2,1,0:T(8,128)(2,1)S(1)}, bf16[1,16,8,960]{3,2,1,0:T(8,128)(2,1)S(1)}, u32[]{:S(2)}, u32[]{:S(2)}) collective-permute-start(bf16[1,16,8,960]{3,2,1,0:T(8,128)(2,1)S(1)} %get-tuple-element.16), channel_id=1, source_target_pairs={{0,13},{1,12},{2,15},{3,14},{4,9},{5,8},{6,11},{7,10},{8,5},{9,4},... | collective-permute-start | bytes 737288 | tf_op jit(solution)/shard_map/ppermute | solution.py:98
  141.3 62.4 %collective-permute-start.28 = (bf16[1,16,8,960]{3,2,1,0:T(8,128)(2,1)S(1)}, bf16[1,16,8,960]{3,2,1,0:T(8,128)(2,1)S(1)}, u32[]{:S(2)}, u32[]{:S(2)}) collective-permute-start(bf16[1,16,8,960]{3,2,1,0:T(8,128)(2,1)S(1)} %get-tuple-element.15), channel_id=1, source_target_pairs={{0,14},{1,15},{2,12},{3,13},{4,10},{5,11},{6,8},{7,9},{8,6},{9,7},... | collective-permute-start | bytes 737288 | tf_op jit(solution)/shard_map/ppermute | solution.py:98
  172.3 37.0 %collective-permute-start.29 = (bf16[1,16,8,960]{3,2,1,0:T(8,128)(2,1)S(1)}, bf16[1,16,8,960]{3,2,1,0:T(8,128)(2,1)S(1)}, u32[]{:S(2)}, u32[]{:S(2)}) collective-permute-start(bf16[1,16,8,960]{3,2,1,0:T(8,128)(2,1)S(1)} %get-tuple-element.14), channel_id=1, source_target_pairs={{0,15},{1,14},{2,13},{3,12},{4,11},{5,10},{6,9},{7,8},{8,7},{9,6},... | collective-permute-start | bytes 737288 | tf_op jit(solution)/shard_map/ppermute | solution.py:98
  215.3 24.4 %collective-permute-start.30 = (bf16[1,16,8,384]{3,2,1,0:T(8,128)(2,1)S(1)}, bf16[1,16,8,384]{3,2,1,0:T(8,128)(2,1)S(1)}, u32[]{:S(2)}, u32[]{:S(2)}) collective-permute-start(bf16[1,16,8,384]{3,2,1,0:T(8,128)(2,1)S(1)} %get-tuple-element.44), channel_id=1, source_target_pairs={{0,1},{1,0},{2,3},{3,2},{4,5},{5,4},{6,7},{7,6},{8,9},{9,8},{10,11... | collective-permute-start | bytes 294920 | tf_op jit(solution)/shard_map/ppermute | solution.py:98
  215.7 24.0 %collective-permute-start.31 = (bf16[1,16,8,384]{3,2,1,0:T(8,128)(2,1)S(1)}, bf16[1,16,8,384]{3,2,1,0:T(8,128)(2,1)S(1)}, u32[]{:S(2)}, u32[]{:S(2)}) collective-permute-start(bf16[1,16,8,384]{3,2,1,0:T(8,128)(2,1)S(1)} %get-tuple-element.43), channel_id=1, source_target_pairs={{0,2},{1,3},{2,0},{3,1},{4,6},{5,7},{6,4},{7,5},{8,10},{9,11},{10,... | collective-permute-start | bytes 294920 | tf_op jit(solution)/shard_map/ppermute | solution.py:98
  215.7 26.8 %collective-permute-start.32 = (bf16[1,16,8,384]{3,2,1,0:T(8,128)(2,1)S(1)}, bf16[1,16,8,384]{3,2,1,0:T(8,128)(2,1)S(1)}, u32[]{:S(2)}, u32[]{:S(2)}) collective-permute-start(bf16[1,16,8,384]{3,2,1,0:T(8,128)(2,1)S(1)} %get-tuple-element.42), channel_id=1, source_target_pairs={{0,3},{1,2},{2,1},{3,0},{4,7},{5,6},{6,5},{7,4},{8,11},{9,10},{10,... | collective-permute-start | bytes 294920 | tf_op jit(solution)/shard_map/ppermute | solution.py:98
  217.5 25.2 %collective-permute-start.33 = (bf16[1,16,8,384]{3,2,1,0:T(8,128)(2,1)S(1)}, bf16[1,16,8,384]{3,2,1,0:T(8,128)(2,1)S(1)}, u32[]{:S(2)}, u32[]{:S(2)}) collective-permute-start(bf16[1,16,8,384]{3,2,1,0:T(8,128)(2,1)S(1)} %get-tuple-element.41), channel_id=1, source_target_pairs={{0,4},{1,5},{2,6},{3,7},{4,0},{5,1},{6,2},{7,3},{8,12},{9,13},{10,... | collective-permute-start | bytes 294920 | tf_op jit(solution)/shard_map/ppermute | solution.py:98
  217.5 27.8 %collective-permute-start.34 = (bf16[1,16,8,384]{3,2,1,0:T(8,128)(2,1)S(1)}, bf16[1,16,8,384]{3,2,1,0:T(8,128)(2,1)S(1)}, u32[]{:S(2)}, u32[]{:S(2)}) collective-permute-start(bf16[1,16,8,384]{3,2,1,0:T(8,128)(2,1)S(1)} %get-tuple-element.40), channel_id=1, source_target_pairs={{0,5},{1,4},{2,7},{3,6},{4,1},{5,0},{6,3},{7,2},{8,13},{9,12},{10,... | collective-permute-start | bytes 294920 | tf_op jit(solution)/shard_map/ppermute | solution.py:98
  245.3 16.9 %collective-permute-start.39 = (bf16[1,16,8,384]{3,2,1,0:T(8,128)(2,1)S(1)}, bf16[1,16,8,384]{3,2,1,0:T(8,128)(2,1)S(1)}, u32[]{:S(2)}, u32[]{:S(2)}) collective-permute-start(bf16[1,16,8,384]{3,2,1,0:T(8,128)(2,1)S(1)} %get-tuple-element.35), channel_id=1, source_target_pairs={{0,10},{1,11},{2,8},{3,9},{4,14},{5,15},{6,12},{7,13},{8,2},{9,3},... | collective-permute-start | bytes 294920 | tf_op jit(solution)/shard_map/ppermute | solution.py:98
  245.4 18.9 %collective-permute-start.40 = (bf16[1,16,8,384]{3,2,1,0:T(8,128)(2,1)S(1)}, bf16[1,16,8,384]{3,2,1,0:T(8,128)(2,1)S(1)}, u32[]{:S(2)}, u32[]{:S(2)}) collective-permute-start(bf16[1,16,8,384]{3,2,1,0:T(8,128)(2,1)S(1)} %get-tuple-element.34), channel_id=1, source_target_pairs={{0,11},{1,10},{2,9},{3,8},{4,15},{5,14},{6,13},{7,12},{8,3},{9,2},... | collective-permute-start | bytes 294920 | tf_op jit(solution)/shard_map/ppermute | solution.py:98
  249.1 23.1 %collective-permute-start.41 = (bf16[1,16,8,384]{3,2,1,0:T(8,128)(2,1)S(1)}, bf16[1,16,8,384]{3,2,1,0:T(8,128)(2,1)S(1)}, u32[]{:S(2)}, u32[]{:S(2)}) collective-permute-start(bf16[1,16,8,384]{3,2,1,0:T(8,128)(2,1)S(1)} %get-tuple-element.33), channel_id=1, source_target_pairs={{0,12},{1,13},{2,14},{3,15},{4,8},{5,9},{6,10},{7,11},{8,4},{9,5},... | collective-permute-start | bytes 294920 | tf_op jit(solution)/shard_map/ppermute | solution.py:98
  249.2 25.3 %collective-permute-start.42 = (bf16[1,16,8,384]{3,2,1,0:T(8,128)(2,1)S(1)}, bf16[1,16,8,384]{3,2,1,0:T(8,128)(2,1)S(1)}, u32[]{:S(2)}, u32[]{:S(2)}) collective-permute-start(bf16[1,16,8,384]{3,2,1,0:T(8,128)(2,1)S(1)} %get-tuple-element.32), channel_id=1, source_target_pairs={{0,13},{1,12},{2,15},{3,14},{4,9},{5,8},{6,11},{7,10},{8,5},{9,4},... | collective-permute-start | bytes 294920 | tf_op jit(solution)/shard_map/ppermute | solution.py:98
  258.0 17.8 %collective-permute-start.43 = (bf16[1,16,8,384]{3,2,1,0:T(8,128)(2,1)S(1)}, bf16[1,16,8,384]{3,2,1,0:T(8,128)(2,1)S(1)}, u32[]{:S(2)}, u32[]{:S(2)}) collective-permute-start(bf16[1,16,8,384]{3,2,1,0:T(8,128)(2,1)S(1)} %get-tuple-element.31), channel_id=1, source_target_pairs={{0,14},{1,15},{2,12},{3,13},{4,10},{5,11},{6,8},{7,9},{8,6},{9,7},... | collective-permute-start | bytes 294920 | tf_op jit(solution)/shard_map/ppermute | solution.py:98
  262.2 16.0 %collective-permute-start.44 = (bf16[1,16,8,384]{3,2,1,0:T(8,128)(2,1)S(1)}, bf16[1,16,8,384]{3,2,1,0:T(8,128)(2,1)S(1)}, u32[]{:S(2)}, u32[]{:S(2)}) collective-permute-start(bf16[1,16,8,384]{3,2,1,0:T(8,128)(2,1)S(1)} %get-tuple-element.30), channel_id=1, source_target_pairs={{0,15},{1,14},{2,13},{3,12},{4,11},{5,10},{6,9},{7,8},{8,7},{9,6},... | collective-permute-start | bytes 294920 | tf_op jit(solution)/shard_map/ppermute | solution.py:98
  (48 other events, 501.1 us)
